TPU v7x, 256 devices: a whole 4x4x8 slice. The times are simulated.
256 devices in a mesh: req: 32 (over x, z), kv: 8 (over y, core).
Axes of the slice: x: 4, y: 4, z: 8, core: 2. Of those that a mesh axis runs over, the one named last changes fastest.
Arguments:
- states: bfloat16 [256, 2560], P(('req', 'kv')), may hold values from -6 to 6
- norm_gain: bfloat16 [2560], replicated, may hold values from 0.099609375 to 1.8984375
- w_query: bfloat16 [2560, 2560], P(None, 'kv'), may hold values from -0.125 to 0.125
- key_projection_weight: bfloat16 [2560, 640], P(None, 'kv'), may hold values from -0.125 to 0.125
- value_projection_weight: bfloat16 [2560, 640], P(None, 'kv'), may hold values from -0.125 to 0.125
- cache_keys: bfloat16 [256, 8, 80, 4096], P('req', 'kv')
- value_cache_slots: bfloat16 [256, 8, 80, 4096], P('req', 'kv'), may hold values from -6 to 6
- lengths: int32 [256], P('req'), may hold values from 1 to 16383, as said below
- write_pos: int32 [256], P('req'), may hold values from 0 to 4095, as said below
- dealing: int32 [256], replicated, may hold values from 0 to 255, each once
Outputs:
- context: bfloat16 [256, 2560], P(('req', 'kv'))
Inputs may be any that keep to these rules, and one draw needn't show every extreme that they name: `lengths`: largest value is reached by some request in every draw. write_pos equals lengths modulo 4096. `dealing`: A permutation of the requests.
All inputs are finite; a program needn't handle non-finite values.
Results may differ from a plain program's by a relative error of at most 0.022.
The roundings to bfloat16 on the way count: a program that leaves them out, or rounds other values in their place, can miss the bound.
Values may be sent and summed in bfloat16 or wider, within the bound.
No kernel may reach another device: no remote copies, remote signals or barrier semaphores. Data moves between devices by JAX's collectives and lax.ppermute only.
A program may use at most 64 MiB of HBM per device.

v0:
```python
import jax
import jax.numpy as jnp
from jax import lax
from jax.sharding import PartitionSpec as P

HEAD_DIMENSION = 80


def apply_rotary(tensor, positions):
    half_width = tensor.shape[-1] // 2
    frequency = 10000.0 ** (-(jnp.arange(half_width, dtype=jnp.float32) * 2.0 / tensor.shape[-1]))
    angles = positions.astype(jnp.float32)[:, None] * frequency[None, :]
    cosine = jnp.cos(angles)[:, None, :]
    sine_part = jnp.sin(angles)[:, None, :]
    front_half = tensor[..., :half_width]
    back_half = tensor[..., half_width:]
    return jnp.concatenate(
        [front_half * cosine - back_half * sine_part, back_half * cosine + front_half * sine_part],
        axis=-1,
    )


def local(
    states,
    norm_gain,
    w_query,
    key_projection_weight,
    value_projection_weight,
    cache_keys,
    value_cache_slots,
    lengths,
    write_pos,
    dealing,
):
    kv_count = lax.axis_size("kv")
    per_device = states.shape[0]
    group_rows = per_device * kv_count
    group_index = lax.axis_index("req")
    kv_index = lax.axis_index("kv")
    req_count = lax.axis_size("req")
    dealt_ids = lax.dynamic_slice_in_dim(dealing, group_index * group_rows, group_rows)
    column_rows = lax.all_gather(states, "req", axis=0, tiled=True)
    column_ids = jnp.arange(req_count, dtype=jnp.int32) * kv_count + kv_index
    pick_in = (dealt_ids[:, None] == column_ids[None, :]).astype(jnp.bfloat16)
    own_part = jnp.dot(pick_in, column_rows, preferred_element_type=jnp.float32).astype(
        jnp.bfloat16
    )
    dealt_rows = lax.psum(own_part, "kv")
    wide_rows = dealt_rows.astype(jnp.float32)
    inv_rms = lax.rsqrt(jnp.mean(wide_rows * wide_rows, axis=1, keepdims=True) + 1e-05)
    normalized_input = (wide_rows * inv_rms * norm_gain.astype(jnp.float32)[None, :]).astype(
        jnp.bfloat16
    )
    head_size = HEAD_DIMENSION
    heads_dev = key_projection_weight.shape[1] // head_size
    queries_per_group = w_query.shape[1] // key_projection_weight.shape[1]
    window_size = cache_keys.shape[3]
    query_vectors = jnp.dot(normalized_input, w_query, preferred_element_type=jnp.float32).reshape(
        group_rows, heads_dev * queries_per_group, head_size
    )
    query_vectors = (
        apply_rotary(query_vectors, lengths)
        .astype(jnp.bfloat16)
        .reshape(group_rows, heads_dev, queries_per_group, head_size)
    )
    fresh_key_rows = jnp.dot(
        normalized_input, key_projection_weight, preferred_element_type=jnp.float32
    ).reshape(group_rows, heads_dev, head_size)
    fresh_key_rows = apply_rotary(fresh_key_rows, lengths).astype(jnp.bfloat16)
    fresh_value_rows = (
        jnp.dot(normalized_input, value_projection_weight, preferred_element_type=jnp.float32)
        .astype(jnp.bfloat16)
        .reshape(group_rows, heads_dev, head_size)
    )
    score_scale = 1.0 / head_size**0.5
    scores = (
        jnp.einsum("rkgh,rkhw->rkgw", query_vectors, cache_keys, preferred_element_type=jnp.float32)
        * score_scale
    )
    own_score = (
        jnp.einsum(
            "rkgh,rkh->rkg", query_vectors, fresh_key_rows, preferred_element_type=jnp.float32
        )
        * score_scale
    )
    slot_ids = lax.broadcasted_iota(jnp.int32, (group_rows, 1, 1, window_size), 3)
    at_write = slot_ids == write_pos[:, None, None, None]
    scores = jnp.where(at_write, own_score[..., None], scores)
    scores = jnp.where(slot_ids <= lengths[:, None, None, None], scores, -jnp.inf)
    row_max = jnp.max(scores, axis=-1, keepdims=True)
    expd = jnp.exp(scores - row_max)
    softmax_weights = (expd / jnp.sum(expd, axis=-1, keepdims=True)).astype(jnp.bfloat16)
    stale_weights = jnp.where(at_write, jnp.zeros((), jnp.bfloat16), softmax_weights)
    fresh_weight = jnp.sum(
        jnp.where(at_write, softmax_weights, jnp.zeros((), jnp.bfloat16)).astype(jnp.float32),
        axis=-1,
    )
    mixed = jnp.einsum(
        "rkgw,rkhw->rkgh", stale_weights, value_cache_slots, preferred_element_type=jnp.float32
    )
    mixed = mixed + fresh_weight[..., None] * fresh_value_rows[:, :, None, :].astype(jnp.float32)
    attended = mixed.reshape(group_rows, heads_dev * queries_per_group * head_size).astype(
        jnp.bfloat16
    )
    group_context = lax.all_gather(attended, "kv", axis=1, tiled=True)
    pick_out = (column_ids[:, None] == dealt_ids[None, :]).astype(jnp.bfloat16)
    routed = jnp.dot(pick_out, group_context, preferred_element_type=jnp.float32).astype(
        jnp.bfloat16
    )
    result = lax.psum_scatter(routed, "req", scatter_dimension=0, tiled=True)
    return result


def solution(mesh):
    in_specs = (
        P(("req", "kv"), None),
        P(),
        P(None, "kv"),
        P(None, "kv"),
        P(None, "kv"),
        P("req", "kv", None, None),
        P("req", "kv", None, None),
        P("req"),
        P("req"),
        P(),
    )
    out_specs = P(("req", "kv"), None)
    return jax.shard_map(local, mesh=mesh, in_specs=in_specs, out_specs=out_specs, check_vma=False)
```

profile of v0, /device:TPU:8, one launch (start us, length us, event | category | flops | bytes accessed | tf_op | source)
XLA Modules:
  0.0 262.5 jit_solution(17877185251697256283)
XLA Ops:
  6.5 0.0 copy-start
  6.5 0.0 all-reduce.3.cloned.1.call-start
  6.6 0.8 convert_element_type.54
  7.3 0.7 iota_compare_fusion
  8.1 0.7 convert_element_type.52
  8.8 0.7 iota_compare_fusion.1
  9.5 52.7 %all-gather = bf16[32,1,2560]{2,1,0:T(2,128)(2,1)S(1)} all-gather(bf16[1,1,2560]{2,1,0:T(2,128)(2,1)} %bitcast.43), channel_id=1, replica_groups=mesh['req'=32,'kv'=8] {'req'}, dimensions={0}, use_global_device_ids=true | all-gather | bytes 168960 | tf_op jit(solution)/shard_map/all_gather | solution.py:42
  62.3 0.8 dynamic_slice.3
  63.0 0.2 convolution_convert_fusion.1
  63.2 21.0 %psum.7 = bf16[8,2560]{1,0:T(8,128)(2,1)S(1)} all-reduce(bf16[8,2560]{1,0:T(8,128)(2,1)S(1)} %convolution_convert_fusion.1), channel_id=1, replica_groups=mesh['req'=32,'kv'=8] {'kv'}, use_global_device_ids=true, to_apply=%region_0.0 | all-reduce | flops 20480 | bytes 81920 | tf_op jit(solution)/shard_map/psum | solution.py:48
  84.2 0.1 fusion.28
  84.4 0.1 multiply_cosine_fusion.1
  84.5 1.3 convolution_bitcast_fusion
  85.7 0.1 fusion.48
  85.9 1.3 fusion.22
  87.1 0.0 copy-done
  87.1 0.5 fusion.52
  87.7 0.1 reshape.241
  87.7 0.1 maximum_bitcast_fusion
  87.8 0.1 subtract_convert_fusion
  87.9 0.2 fusion.43
  88.1 0.0 copy-start.1
  88.1 3.7 %fusion.54 = (f32[8,4]{1,0:T(8,128)S(1)}, f32[8,4,4096]{2,1,0:T(4,128)S(1)}) fusion(bf16[8,1,80,4096]{3,2,1,0:T(8,128)(2,1)} %param.15, f32[8,4]{1,0:T(8,128)S(1)} %broadcast_multiply_fusion, pred[8,4096]{1,0:T(8,128)(4,1)S(1)} %iota_compare_fusion, pred[8,4096]{1,0:T(8,128)(4,1)S(1)} %iota_compare_fusion.1, bf16[8,4,40]{2,1,0:T(4,128)(2,1)S(1)} %get-tuple-element.8, ...), kind=kOutput, calls=%fused_computation.64 | convolution fusion | flops 21641216 | bytes 5838080 | tf_op jit(solution)/shard_map/sub | solution.py:91
  91.8 0.4 convert_reduce_fusion
  92.2 4.0 %fusion.19 = bf16[8,4,80]{2,1,0:T(4,128)(2,1)S(1)} fusion(bf16[8,1,80,4096]{3,2,1,0:T(8,128)(2,1)} %param.16, bf16[8,4,4096]{2,1,0:T(4,128)(2,1)S(1)} %get-tuple-element.6, pred[8,4096]{1,0:T(8,128)(4,1)S(1)} %iota_compare_fusion.1, f32[8,80]{1,0:T(8,128)S(1)} %fusion.22, f32[8,4]{1,0:T(8,128)S(1)} %get-tuple-element.5), kind=kOutput, calls=%fused_computation.13 | convolution fusion | flops 21110272 | bytes 5545600 | tf_op jit(solution)/shard_map/rkgw,rkhw->rkgh/dot_general | solution.py:98
  96.1 0.1 convert_element_type.60
  96.2 13.1 %all-gather.1 = bf16[8,320,8]{1,2,0:T(8,128)(2,1)S(1)} all-gather(bf16[1,320,8]{1,2,0:T(8,128)(2,1)S(1)} %bitcast.42), channel_id=1, replica_groups=mesh['req'=32,'kv'=8] {'kv'}, dimensions={0}, use_global_device_ids=true | all-gather | bytes 46080 | tf_op jit(solution)/shard_map/all_gather | solution.py:105
  109.4 0.1 reshape.248
  109.5 0.9 convolution_convert_fusion
  110.4 0.0 all-reduce.3.cloned.1.call-update
  110.4 0.0 copy-done.1
  110.4 0.7 dynamic-slice
  111.1 142.5 %all-reduce.3.cloned.1.call-done = bf16[32,2560]{1,0:T(8,128)(2,1)} async-done(((bf16[32,2560]{1,0:T(8,128)(2,1)}), bf16[32,2560]{1,0:T(8,128)(2,1)}) %all-reduce.3.cloned.1.call-update) | async-done | bytes 163856
  253.6 2.1 constant_dynamic-slice_fusion
  (5 shorter events, 0.0 us)
Async XLA Ops:
  6.5 80.6 %copy-start = (bf16[2560,320]{0,1:T(8,128)(2,1)S(1)}, bf16[2560,320]{0,1:T(8,128)(2,1)}, u32[]{:S(2)}) copy-start(bf16[2560,320]{0,1:T(8,128)(2,1)} %param.12) | copy-start | bytes 4915204
  6.5 247.0 %all-reduce.3.cloned.1.call-start = ((), (), s32[]{:S(2)}) async-start(), calls=%async_computation | async-start | bytes 327680
  88.1 22.3 %copy-start.1 = (u32[256]{0:T(256)S(1)}, u32[256]{0:T(256)}, u32[]{:S(2)}) copy-start(u32[256]{0:T(256)} %constant.44) | copy-start | bytes 3076
Sparse Core Ops, SparseCore 0:
  110.5 142.9 all-reduce.2
where the time goes:
time: 263 us; the launch traced here: 262 us
  waiting for transfers between devices  143 us (54%)
  blocking collectives  86.9 us (33%)
  between operations  13.5 us (5%)
  matrix products  12 us (5%)
  other arithmetic  3.91 us (1%)
  local copies, waits for them, and re-layouts  3.79 us (1%)
    unnamed x2, waiting for transfers between devices  143 us
    all_gather x1, blocking collectives, local(): column_rows = lax.all_gather(states, 'req', axis=0, tiled=True)  52.7 us
    psum x1, blocking collectives, local(): dealt_rows = lax.psum(own_part, 'kv')  21 us
    all_gather x1, blocking collectives, local(): group_context = lax.all_gather(attended, 'kv', axis=1, tiled=True)  13.1 us
  transfers between devices with their start and end apart: 1, of which 1 were waited for; matrix products, arithmetic and copies ran while one was open for 0% of the time, Pallas kernels for 0%

commit v1 on v0

--- a/solution.py
+++ b/solution.py
@@ -102,7 +102,10 @@
     attended = mixed.reshape(group_rows, heads_dev * queries_per_group * head_size).astype(
         jnp.bfloat16
     )
-    group_context = lax.all_gather(attended, "kv", axis=1, tiled=True)
+    n_dev = lax.axis_size("kv")
+    blocks = jnp.stack([attended for _ in range(n_dev)])
+    blocks = lax.all_to_all(blocks, "kv", split_axis=0, concat_axis=0)
+    group_context = jnp.concatenate(blocks, axis=1)
     pick_out = (column_ids[:, None] == dealt_ids[None, :]).astype(jnp.bfloat16)
     routed = jnp.dot(pick_out, group_context, preferred_element_type=jnp.float32).astype(
         jnp.bfloat16

time: 263 us -> 258 us (0.981)
  blocking collectives: 86.9 us -> 83.7 us
  waiting for transfers between devices: 143 us -> 140 us
    all_gather x1 -> x0, blocking collectives: 13.1 us -> none  [local(): group_context = lax.all_gather(attended, 'kv', axis=1, tiled=True)]
    all_to_all x0 -> x1, blocking collectives: none -> 9.96 us  [local(): blocks = lax.all_to_all(blocks, 'kv', split_axis=0, concat_axis=0)]
where the time goes in v1:
time: 258 us; the launch traced here: 257 us
  waiting for transfers between devices  140 us (54%)
  blocking collectives  83.7 us (32%)
  between operations  13.5 us (5%)
  matrix products  12 us (5%)
  other arithmetic  3.91 us (2%)
  local copies, waits for them, and re-layouts  3.8 us (1%)
    unnamed x2, waiting for transfers between devices  140 us
    all_gather x1, blocking collectives, local(): column_rows = lax.all_gather(states, 'req', axis=0, tiled=True)  52.7 us
    psum x1, blocking collectives, local(): dealt_rows = lax.psum(own_part, 'kv')  21 us
    all_to_all x1, blocking collectives, local(): blocks = lax.all_to_all(blocks, 'kv', split_axis=0, concat_axis=0)  9.96 us
  transfers between devices with their start and end apart: 1, of which 1 were waited for; matrix products, arithmetic and copies ran while one was open for 0% of the time, Pallas kernels for 0%

profile of v1, /device:TPU:8, one launch (start us, length us, event | category | flops | bytes accessed | tf_op | source)
XLA Modules:
  0.0 257.2 jit_solution(11078923148430858313)
XLA Ops:
  6.5 0.0 copy-start
  6.5 0.0 all-reduce.3.cloned.1.call-start
  6.6 0.8 convert_element_type.56
  7.3 0.7 iota_compare_fusion
  8.1 0.7 convert_element_type.54
  8.8 0.7 iota_compare_fusion.1
  9.5 52.7 %all-gather = bf16[32,1,2560]{2,1,0:T(2,128)(2,1)S(1)} all-gather(bf16[1,1,2560]{2,1,0:T(2,128)(2,1)} %bitcast.39), channel_id=1, replica_groups=mesh['req'=32,'kv'=8] {'req'}, dimensions={0}, use_global_device_ids=true | all-gather | bytes 168960 | tf_op jit(solution)/shard_map/all_gather | solution.py:42
  62.3 0.8 dynamic_slice.3
  63.0 0.2 convolution_convert_fusion.1
  63.2 21.0 %psum.7 = bf16[8,2560]{1,0:T(8,128)(2,1)S(1)} all-reduce(bf16[8,2560]{1,0:T(8,128)(2,1)S(1)} %convolution_convert_fusion.1), channel_id=1, replica_groups=mesh['req'=32,'kv'=8] {'kv'}, use_global_device_ids=true, to_apply=%region_0.0 | all-reduce | flops 20480 | bytes 81920 | tf_op jit(solution)/shard_map/psum | solution.py:48
  84.2 0.1 fusion.28
  84.4 0.1 multiply_cosine_fusion.1
  84.5 1.3 convolution_bitcast_fusion
  85.7 0.1 fusion.48
  85.9 1.3 fusion.22
  87.1 0.0 copy-done
  87.1 0.5 fusion.52
  87.7 0.1 reshape.250
  87.7 0.1 maximum_bitcast_fusion
  87.8 0.1 subtract_convert_fusion
  87.9 0.2 fusion.43
  88.1 0.0 copy-start.1
  88.1 3.7 %fusion.54 = (f32[8,4]{1,0:T(8,128)S(1)}, f32[8,4,4096]{2,1,0:T(4,128)S(1)}) fusion(bf16[8,1,80,4096]{3,2,1,0:T(8,128)(2,1)} %param.15, f32[8,4]{1,0:T(8,128)S(1)} %broadcast_multiply_fusion, pred[8,4096]{1,0:T(8,128)(4,1)S(1)} %iota_compare_fusion, pred[8,4096]{1,0:T(8,128)(4,1)S(1)} %iota_compare_fusion.1, bf16[8,4,40]{2,1,0:T(4,128)(2,1)S(1)} %get-tuple-element.8, ...), kind=kOutput, calls=%fused_computation.64 | convolution fusion | flops 21641216 | bytes 5838080 | tf_op jit(solution)/shard_map/sub | solution.py:91
  91.8 0.4 convert_reduce_fusion
  92.2 4.0 %fusion.19 = bf16[8,4,80]{2,1,0:T(4,128)(2,1)S(1)} fusion(bf16[8,1,80,4096]{3,2,1,0:T(8,128)(2,1)} %param.16, bf16[8,4,4096]{2,1,0:T(4,128)(2,1)S(1)} %get-tuple-element.6, pred[8,4096]{1,0:T(8,128)(4,1)S(1)} %iota_compare_fusion.1, f32[8,80]{1,0:T(8,128)S(1)} %fusion.22, f32[8,4]{1,0:T(8,128)S(1)} %get-tuple-element.5), kind=kOutput, calls=%fused_computation.13 | convolution fusion | flops 21110272 | bytes 5545600 | tf_op jit(solution)/shard_map/rkgw,rkhw->rkgh/dot_general | solution.py:98
  96.1 0.1 convert_element_type.62
  96.2 10.0 %all_to_all.5 = bf16[8,8,320]{2,1,0:T(8,128)(2,1)S(1)} all-to-all(bf16[8,8,320]{2,1,0:T(8,128)(2,1)S(1)} %stack.2), channel_id=1, replica_groups=mesh['req'=32,'kv'=8] {'kv'}, dimensions={0} | all-to-all | bytes 81920 | tf_op jit(solution)/shard_map/all_to_all | solution.py:107
  106.2 0.1 reshape.255
  106.3 0.9 convolution_convert_fusion
  107.2 0.0 all-reduce.3.cloned.1.call-update
  107.3 0.0 copy-done.1
  107.3 0.7 dynamic-slice
  107.9 140.4 %all-reduce.3.cloned.1.call-done = bf16[32,2560]{1,0:T(8,128)(2,1)} async-done(((bf16[32,2560]{1,0:T(8,128)(2,1)}), bf16[32,2560]{1,0:T(8,128)(2,1)}) %all-reduce.3.cloned.1.call-update) | async-done | bytes 163856
  248.3 2.1 constant_dynamic-slice_fusion
  (6 shorter events, 0.1 us)
Async XLA Ops:
  6.5 80.6 %copy-start = (bf16[2560,320]{0,1:T(8,128)(2,1)S(1)}, bf16[2560,320]{0,1:T(8,128)(2,1)}, u32[]{:S(2)}) copy-start(bf16[2560,320]{0,1:T(8,128)(2,1)} %param.12) | copy-start | bytes 4915204
  6.5 241.7 %all-reduce.3.cloned.1.call-start = ((), (), s32[]{:S(2)}) async-start(), calls=%async_computation.1 | async-start | bytes 327680
  88.1 19.1 %copy-start.1 = (u32[256]{0:T(256)S(1)}, u32[256]{0:T(256)}, u32[]{:S(2)}) copy-start(u32[256]{0:T(256)} %constant.44) | copy-start | bytes 3076
Sparse Core Ops, SparseCore 0:
  107.4 140.8 all-reduce.2

commit v2 on v0

--- a/solution.py
+++ b/solution.py
@@ -2,6 +2,7 @@
 import jax.numpy as jnp
 from jax import lax
 from jax.sharding import PartitionSpec as P
+from jax.lax import all_gather
 
 HEAD_DIMENSION = 80
 
@@ -45,7 +46,8 @@
     own_part = jnp.dot(pick_in, column_rows, preferred_element_type=jnp.float32).astype(
         jnp.bfloat16
     )
-    dealt_rows = lax.psum(own_part, "kv")
+    halves_fit = lambda work_x, dev_axis: jnp.sum(all_gather(work_x, axis_name=dev_axis), 0)
+    dealt_rows = halves_fit(own_part, "kv")
     wide_rows = dealt_rows.astype(jnp.float32)
     inv_rms = lax.rsqrt(jnp.mean(wide_rows * wide_rows, axis=1, keepdims=True) + 1e-05)
     normalized_input = (wide_rows * inv_rms * norm_gain.astype(jnp.float32)[None, :]).astype(

time: 263 us -> 253 us (0.962)
  blocking collectives: 86.9 us -> 78.7 us
    psum x1 -> x0, blocking collectives: 21 us -> none  [local(): dealt_rows = lax.psum(own_part, 'kv')]
    all_gather x0 -> x1, blocking collectives: none -> 13.1 us  [local(): all_gather(work_x, axis_name=dev_axis)]
where the time goes in v2:
time: 253 us
  waiting for transfers between devices  141 us (56%)
  blocking collectives  78.7 us (31%)
  between operations  13.5 us (5%)
  matrix products  12 us (5%)
  other arithmetic  3.96 us (2%)
  local copies, waits for them, and re-layouts  3.79 us (1%)
    unnamed x2, waiting for transfers between devices  141 us
    all_gather x1, blocking collectives, local(): column_rows = lax.all_gather(states, 'req', axis=0, tiled=True)  52.7 us
    all_gather x1, blocking collectives, local(): all_gather(work_x, axis_name=dev_axis)  13.1 us
    all_gather x1, blocking collectives, local(): group_context = lax.all_gather(attended, 'kv', axis=1, tiled=True)  12.8 us
  transfers between devices with their start and end apart: 1, of which 1 were waited for; matrix products, arithmetic and copies ran while one was open for 0% of the time, Pallas kernels for 0%

profile of v2, /device:TPU:8, one launch (start us, length us, event | category | flops | bytes accessed | tf_op | source)
XLA Modules:
  0.0 252.9 jit_solution(8552446818918485788)
XLA Ops:
  6.5 0.0 copy-start
  6.5 0.0 all-reduce.3.cloned.1.call-start
  6.6 0.8 convert_element_type.56
  7.3 0.7 iota_compare_fusion
  8.1 0.7 convert_element_type.54
  8.8 0.7 iota_compare_fusion.1
  9.5 52.7 %all-gather.1 = bf16[32,1,2560]{2,1,0:T(2,128)(2,1)S(1)} all-gather(bf16[1,1,2560]{2,1,0:T(2,128)(2,1)} %bitcast.45), channel_id=1, replica_groups=mesh['req'=32,'kv'=8] {'req'}, dimensions={0}, use_global_device_ids=true | all-gather | bytes 168960 | tf_op jit(solution)/shard_map/all_gather | solution.py:43
  62.3 0.8 dynamic_slice.3
  63.0 0.2 convolution_convert_fusion.1
  63.2 13.1 %all-gather = bf16[64,2560]{1,0:T(8,128)(2,1)S(1)} all-gather(bf16[8,2560]{1,0:T(8,128)(2,1)S(1)} %convolution_convert_fusion.1), channel_id=2, replica_groups=mesh['req'=32,'kv'=8] {'kv'}, dimensions={0}, use_global_device_ids=true | all-gather | bytes 368640 | tf_op jit(solution)/shard_map/all_gather | solution.py:49
  76.4 0.1 fusion.28
  76.5 0.1 multiply_cosine_fusion.1
  76.6 1.3 convolution_bitcast_fusion
  77.9 0.1 fusion.48
  78.0 1.3 fusion.22
  79.3 0.0 copy-done
  79.3 0.5 fusion.52
  79.8 0.1 reshape.241
  79.9 0.1 maximum_bitcast_fusion
  80.0 0.1 subtract_convert_fusion
  80.1 0.2 fusion.43
  80.3 0.0 copy-start.1
  80.3 3.7 %fusion.54 = (f32[8,4]{1,0:T(8,128)S(1)}, f32[8,4,4096]{2,1,0:T(4,128)S(1)}) fusion(bf16[8,1,80,4096]{3,2,1,0:T(8,128)(2,1)} %param.15, f32[8,4]{1,0:T(8,128)S(1)} %broadcast_multiply_fusion, pred[8,4096]{1,0:T(8,128)(4,1)S(1)} %iota_compare_fusion, pred[8,4096]{1,0:T(8,128)(4,1)S(1)} %iota_compare_fusion.1, bf16[8,4,40]{2,1,0:T(4,128)(2,1)S(1)} %get-tuple-element.8, ...), kind=kOutput, calls=%fused_computation.65 | convolution fusion | flops 21641216 | bytes 5838080 | tf_op jit(solution)/shard_map/sub | solution.py:93
  84.0 0.4 convert_reduce_fusion
  84.4 4.0 %fusion.19 = bf16[8,4,80]{2,1,0:T(4,128)(2,1)S(1)} fusion(bf16[8,1,80,4096]{3,2,1,0:T(8,128)(2,1)} %param.16, bf16[8,4,4096]{2,1,0:T(4,128)(2,1)S(1)} %get-tuple-element.6, pred[8,4096]{1,0:T(8,128)(4,1)S(1)} %iota_compare_fusion.1, f32[8,80]{1,0:T(8,128)S(1)} %fusion.22, f32[8,4]{1,0:T(8,128)S(1)} %get-tuple-element.5), kind=kOutput, calls=%fused_computation.13 | convolution fusion | flops 21110272 | bytes 5545600 | tf_op jit(solution)/shard_map/rkgw,rkhw->rkgh/dot_general | solution.py:100
  88.3 0.1 convert_element_type.62
  88.4 12.8 %all-gather.2 = bf16[8,320,8]{1,2,0:T(8,128)(2,1)S(1)} all-gather(bf16[1,320,8]{1,2,0:T(8,128)(2,1)S(1)} %bitcast.44), channel_id=1, replica_groups=mesh['req'=32,'kv'=8] {'kv'}, dimensions={0}, use_global_device_ids=true | all-gather | bytes 46080 | tf_op jit(solution)/shard_map/all_gather | solution.py:107
  101.2 0.1 reshape.249
  101.3 0.9 convolution_convert_fusion
  102.2 0.0 all-reduce.3.cloned.1.call-update
  102.2 0.0 copy-done.1
  102.3 0.7 dynamic-slice
  102.9 141.1 %all-reduce.3.cloned.1.call-done = bf16[32,2560]{1,0:T(8,128)(2,1)} async-done(((bf16[32,2560]{1,0:T(8,128)(2,1)}), bf16[32,2560]{1,0:T(8,128)(2,1)}) %all-reduce.3.cloned.1.call-update) | async-done | bytes 163856
  244.0 2.1 constant_dynamic-slice_fusion
  (6 shorter events, 0.1 us)
Async XLA Ops:
  6.5 72.8 %copy-start = (bf16[2560,320]{0,1:T(8,128)(2,1)S(1)}, bf16[2560,320]{0,1:T(8,128)(2,1)}, u32[]{:S(2)}) copy-start(bf16[2560,320]{0,1:T(8,128)(2,1)} %param.12) | copy-start | bytes 4915204
  6.5 237.5 %all-reduce.3.cloned.1.call-start = ((), (), s32[]{:S(2)}) async-start(), calls=%async_computation | async-start | bytes 327680
  80.3 21.9 %copy-start.1 = (u32[256]{0:T(256)S(1)}, u32[256]{0:T(256)}, u32[]{:S(2)}) copy-start(u32[256]{0:T(256)} %constant.45) | copy-start | bytes 3076
Sparse Core Ops, SparseCore 0:
  102.4 141.6 all-reduce.2
